TPU v7x, 256 devices: a whole 4x4x8 slice. The times are simulated.
256 devices in a mesh: feeder: 32 (over z_hi, y, core), factor: 8 (over z_lo, x).
Axes of the slice: x: 4, y: 4, z: 8 (z_hi: 4, z_lo: 2; z = z_hi * 2 + z_lo), core: 2. Of those that a mesh axis runs over, the one named last changes fastest.
Arguments:
- sensitivity: bfloat16 [32, 2048, 2048], P('feeder'), may hold values from -0.015625 to 0.015625
- headroom: float32 [32, 8, 2048], P('feeder'), may hold values from 0 to 3
- ev_power: float32 [32, 8, 256], P('feeder'), may hold values from 0.5 to 4
- ev_node: int32 [32, 8, 256], P('feeder'), may hold values from 0 to 2047
- region_map: int32 [32, 256], P('feeder'), may hold values from 0 to 511
- loadings: float32 [512, 8, 512], P('feeder', None, 'factor'), may hold values from -8 to 8
Outputs:
- margin: float32 [32, 8, 2048], P('feeder')
- new_loadings: float32 [512, 8, 512], P('feeder', None, 'factor')
All inputs are finite; a program needn't handle non-finite values.
Results may differ from a plain program's by a relative error of at most 0.0031.
Values may be sent and summed in bfloat16 or wider, within the bound.
No kernel may reach another device: no remote copies, remote signals or barrier semaphores. Data moves between devices by JAX's collectives and lax.ppermute only.
A program may use at most 64 MiB of HBM per device.

v0:
```python
import jax
import jax.numpy as jnp
from jax import lax
from jax.sharding import PartitionSpec as P

quantile = 1.645
epsilon = 1e-06
step_size = 16.0


def shards(sensitivity, headroom, ev_power, ev_node, region_map, loadings):
    members = sensitivity.shape[0]
    ev_count = ev_power.shape[2]
    reg_local, hours, columns = loadings.shape
    total_regions = reg_local * lax.axis_size("feeder")
    packed = loadings.astype(jnp.bfloat16).reshape(reg_local, hours * columns)
    regions = region_map.reshape(-1)
    shard_rows = lax.all_gather(packed, "feeder", axis=0, tiled=True)
    row_count = shard_rows.shape[0]
    matches = (regions[:, None] == lax.iota(jnp.int32, row_count)[None, :]).astype(jnp.bfloat16)
    looked = jnp.dot(matches, shard_rows, preferred_element_type=jnp.float32)
    volts_list = []
    rows_list = []
    partial_list = []
    member = 0
    for interval in range(hours):
        block = looked[
            member * ev_count : (member + 1) * ev_count,
            interval * columns : (interval + 1) * columns,
        ]
        weighted = (ev_power[member, interval][:, None] * block).astype(jnp.bfloat16)
        sens_rows = jnp.take(sensitivity[member], ev_node[member, interval], axis=0)
        factor_volts = jnp.dot(weighted.T, sens_rows, preferred_element_type=jnp.float32)
        volts_list.append(factor_volts)
        rows_list.append(sens_rows)
        partial_sum = jnp.sum(factor_volts * factor_volts, axis=0)
        partial_list.append(partial_sum)
    variance = jnp.stack(partial_list, axis=0).reshape(members, hours, -1)
    variance = lax.psum(variance, "factor")
    deviation = jnp.sqrt(variance + epsilon)
    margin = headroom - quantile * deviation
    violation = jnp.maximum(-margin, 0.0)
    var_grad = quantile * violation / deviation
    member = 0
    interval_grads = []
    for interval in range(hours):
        position = member * hours + interval
        volt_grad = (2.0 * var_grad[member, interval][None, :] * volts_list[position]).astype(
            jnp.bfloat16
        )
        weight_grad = jnp.dot(rows_list[position], volt_grad.T, preferred_element_type=jnp.float32)
        interval_grads.append(ev_power[member, interval][:, None] * weight_grad)
    member_grads = jnp.concatenate(interval_grads, axis=1)
    offset = regions - 0
    inside = jnp.logical_and(offset >= 0, offset < total_regions)
    target = jnp.where(inside, offset, total_regions)
    summed = jax.ops.segment_sum(member_grads, target, num_segments=total_regions + 1)
    whole_term = summed[:total_regions]
    reduced = lax.psum_scatter(whole_term, "feeder", scatter_dimension=0, tiled=True)
    new_loadings = loadings - step_size * reduced.reshape(reg_local, hours, columns)
    return (margin, new_loadings)


def solution(mesh):
    return jax.shard_map(
        shards,
        mesh=mesh,
        in_specs=(
            P("feeder", None, None),
            P("feeder", None, None),
            P("feeder", None, None),
            P("feeder", None, None),
            P("feeder", None),
            P("feeder", None, "factor"),
        ),
        out_specs=(P("feeder", None, None), P("feeder", None, "factor")),
        check_vma=False,
    )
```

profile of v0, /device:TPU:2, one launch (start us, length us, event | category | flops | bytes accessed | tf_op | source)
XLA Modules:
  0.0 324.0 jit_solution(15895754559689770932)
XLA Ops:
  7.2 1.0 fusion.61
  8.4 1.0 fusion.60
  9.4 0.8 convert_element_type.52
  10.4 49.2 %all_gather.3 = bf16[512,512]{1,0:T(8,128)(2,1)S(1)} all-gather(bf16[16,512]{1,0:T(8,128)(2,1)S(1)} %reshape.133), channel_id=1, replica_groups=mesh['feeder'=32,'factor'=8] {'feeder'}, dimensions={0}, use_global_device_ids=true | all-gather | bytes 540672 | tf_op jit(solution)/shard_map/all_gather | solution.py:18
  59.6 6.8 %gather_fusion.2 = bf16[256,2048]{1,0:T(8,128)(2,1)S(1)} fusion(bf16[2048,2048]{1,0:T(8,128)(2,1)} %bitcast.39, s32[1024]{0:T(1024)S(1)} %pad_clamp_fusion.5), kind=kCustom, calls=%fused_computation.2.clone | custom fusion | bytes 2098176 | tf_op jit(solution)/shard_map/jit(_take)/gather | solution.py:32
  66.4 6.8 %gather_fusion.3 = bf16[256,2048]{1,0:T(8,128)(2,1)S(1)} fusion(bf16[2048,2048]{1,0:T(8,128)(2,1)} %bitcast.40, s32[1024]{0:T(1024)S(1)} %pad_clamp_fusion.4), kind=kCustom, calls=%fused_computation.3.clone | custom fusion | bytes 2098176 | tf_op jit(solution)/shard_map/jit(_take)/gather | solution.py:32
  73.3 7.8 %gather_fusion.4 = bf16[256,2048]{1,0:T(8,128)(2,1)} fusion(bf16[2048,2048]{1,0:T(8,128)(2,1)} %bitcast.41, s32[1024]{0:T(1024)S(1)} %pad_clamp_fusion.3), kind=kCustom, calls=%fused_computation.4.clone | custom fusion | bytes 2098176 | tf_op jit(solution)/shard_map/jit(_take)/gather | solution.py:32
  81.1 8.0 %gather_fusion.5 = bf16[256,2048]{1,0:T(8,128)(2,1)} fusion(bf16[2048,2048]{1,0:T(8,128)(2,1)} %bitcast.42, s32[1024]{0:T(1024)S(1)} %pad_clamp_fusion.2), kind=kCustom, calls=%fused_computation.5.clone | custom fusion | bytes 2098176 | tf_op jit(solution)/shard_map/jit(_take)/gather | solution.py:32
  89.1 7.8 %gather_fusion.6 = bf16[256,2048]{1,0:T(8,128)(2,1)} fusion(bf16[2048,2048]{1,0:T(8,128)(2,1)} %bitcast.43, s32[1024]{0:T(1024)S(1)} %pad_clamp_fusion.1), kind=kCustom, calls=%fused_computation.6.clone | custom fusion | bytes 2098176 | tf_op jit(solution)/shard_map/jit(_take)/gather | solution.py:32
  96.9 7.8 %gather_fusion.7 = bf16[256,2048]{1,0:T(8,128)(2,1)} fusion(bf16[2048,2048]{1,0:T(8,128)(2,1)} %bitcast.44, s32[1024]{0:T(1024)S(1)} %pad_clamp_fusion), kind=kCustom, calls=%fused_computation.7.clone | custom fusion | bytes 2098176 | tf_op jit(solution)/shard_map/jit(_take)/gather | solution.py:32
  104.7 7.9 %gather_fusion.1 = bf16[256,2048]{1,0:T(8,128)(2,1)} fusion(bf16[2048,2048]{1,0:T(8,128)(2,1)} %bitcast.45, s32[1024]{0:T(1024)S(1)} %pad_clamp_fusion.6), kind=kCustom, calls=%fused_computation.1.clone | custom fusion | bytes 2098176 | tf_op jit(solution)/shard_map/jit(_take)/gather | solution.py:32
  112.6 8.0 %gather_fusion = bf16[256,2048]{1,0:T(8,128)(2,1)} fusion(bf16[2048,2048]{1,0:T(8,128)(2,1)} %bitcast.46, s32[1024]{0:T(1024)S(1)} %pad_clamp_fusion.7), kind=kCustom, calls=%fused_computation.clone | custom fusion | bytes 2098176 | tf_op jit(solution)/shard_map/jit(_take)/gather | solution.py:32
  121.0 1.2 multiply_reduce_fusion.5
  122.2 1.2 multiply_reduce_fusion.4
  123.5 2.5 multiply_reduce_fusion.3
  126.0 2.6 multiply_reduce_fusion.2
  128.5 2.4 multiply_reduce_fusion.1
  131.0 1.3 multiply_reduce_fusion
  132.2 1.3 multiply_reduce_fusion.6
  133.5 1.2 multiply_reduce_fusion.7
  135.6 71.0 %all-reduce.2.cloned.1.call-done = f32[1,8,2048]{2,1,0:T(8,128)} async-done(((f32[1,8,2048]{2,1,0:T(8,128)}), f32[1,8,2048]{2,1,0:T(8,128)}) %all-reduce.2.cloned.1.call-update) | async-done | bytes 65552 | tf_op jit(solution)/shard_map/psum | solution.py:39
  206.6 1.6 multiply_divide_fusion
  208.3 2.0 convolution_multiply_fusion
  210.2 1.8 convolution_multiply_fusion.1
  212.1 2.5 convolution_multiply_fusion.2
  214.5 2.5 convolution_multiply_fusion.3
  217.1 1.1 convolution_multiply_fusion.4
  219.8 1.3 concatenate.3
  221.1 2.3 scatter_custom_fusion
  223.4 1.1 slice.172
  224.5 91.1 %reduce-scatter.2.cloned.1.call-done = f32[16,512]{1,0:T(8,128)} async-done(((f32[512,512]{1,0:T(8,128)}), f32[16,512]{1,0:T(8,128)}) %reduce-scatter.2.cloned.1.call-update) | async-done | bytes 32784 | tf_op jit(solution)/shard_map/reduce_scatter | solution.py:59
  315.6 0.8 broadcast_multiply_fusion
  (62 shorter events, 3.7 us)
Async XLA Ops:
  7.2 199.4 %all-reduce.2.cloned.1.call-start = ((), (), s32[]{:S(2)}) async-start(), calls=%async_computation.1 | async-start | bytes 131072 | tf_op jit(solution)/shard_map/psum | solution.py:39
  104.7 15.9 %copy-start.7 = (s32[1,256]{1,0:T(1,128)S(1)}, s32[1,256]{1,0:T(1,128)}, u32[]{:S(2)}) copy-start(s32[1,256]{1,0:T(1,128)} %param.12) | copy-start | bytes 3076
  120.6 10.4 %copy-start.4 = (bf16[256,2048]{1,0:T(8,128)(2,1)S(1)}, bf16[256,2048]{1,0:T(8,128)(2,1)}, u32[]{:S(2)}) copy-start(bf16[256,2048]{1,0:T(8,128)(2,1)} %gather_fusion.7) | copy-start | bytes 3145732
  120.6 11.6 %copy-start.2 = (bf16[256,2048]{1,0:T(8,128)(2,1)S(1)}, bf16[256,2048]{1,0:T(8,128)(2,1)}, u32[]{:S(2)}) copy-start(bf16[256,2048]{1,0:T(8,128)(2,1)} %gather_fusion.1) | copy-start | bytes 3145732
  120.6 12.9 %copy-start = (bf16[256,2048]{1,0:T(8,128)(2,1)S(1)}, bf16[256,2048]{1,0:T(8,128)(2,1)}, u32[]{:S(2)}) copy-start(bf16[256,2048]{1,0:T(8,128)(2,1)} %gather_fusion) | copy-start | bytes 3145732
  120.6 85.9 %copy-start.6 = (f32[1,8,2048]{2,1,0:T(8,128)S(1)}, f32[1,8,2048]{2,1,0:T(8,128)}, u32[]{:S(2)}) copy-start(f32[1,8,2048]{2,1,0:T(8,128)} %param.9) | copy-start | bytes 196612
  133.5 85.2 %copy-start.3 = (bf16[256,2048]{1,0:T(8,128)(2,1)S(1)}, bf16[256,2048]{1,0:T(8,128)(2,1)}, u32[]{:S(2)}) copy-start(bf16[256,2048]{1,0:T(8,128)(2,1)} %gather_fusion.1) | copy-start | bytes 3145732
  135.5 180.1 %reduce-scatter.2.cloned.1.call-start = ((), (), s32[]{:S(2)}) async-start(), calls=%async_computation.2 | async-start | bytes 1081344 | tf_op jit(solution)/shard_map/reduce_scatter | solution.py:59
  206.5 10.5 %copy-start.10 = (f32[64,2048]{1,0:T(8,128)S(1)}, f32[64,2048]{1,0:T(8,128)}, u32[]{:S(2)}) copy-start(f32[64,2048]{1,0:T(8,128)} %get-tuple-element.36) | copy-start | bytes 1572868
  206.5 11.7 %copy-start.8 = (f32[64,2048]{1,0:T(8,128)S(1)}, f32[64,2048]{1,0:T(8,128)}, u32[]{:S(2)}) copy-start(f32[64,2048]{1,0:T(8,128)} %get-tuple-element.34) | copy-start | bytes 1572868
  206.5 12.2 %copy-start.11 = (f32[64,2048]{1,0:T(8,128)S(1)}, f32[64,2048]{1,0:T(8,128)}, u32[]{:S(2)}) copy-start(f32[64,2048]{1,0:T(8,128)} %get-tuple-element.32) | copy-start | bytes 1572868
  208.2 11.0 %copy-start.1 = (bf16[256,2048]{1,0:T(8,128)(2,1)S(1)}, bf16[256,2048]{1,0:T(8,128)(2,1)}, u32[]{:S(2)}) copy-start(bf16[256,2048]{1,0:T(8,128)(2,1)} %gather_fusion) | copy-start | bytes 3145732
  208.2 11.0 %copy-start.9 = (f32[64,2048]{1,0:T(8,128)S(1)}, f32[64,2048]{1,0:T(8,128)}, u32[]{:S(2)}) copy-start(f32[64,2048]{1,0:T(8,128)} %get-tuple-element.30) | copy-start | bytes 1572868
  214.5 101.9 %copy-start.5 = (f32[16,8,64]{2,1,0:T(8,128)S(1)}, f32[16,8,64]{2,1,0:T(8,128)}, u32[]{:S(2)}) copy-start(f32[16,8,64]{2,1,0:T(8,128)} %param.13) | copy-start | bytes 98308
Sparse Core Ops, SparseCore 0:
  135.6 70.8 all-reduce.1
  224.6 90.9 reduce-scatter.1
where the time goes:
time: 325 us; the launch traced here: 324 us
  waiting for transfers between devices  162 us (50%)
  local copies, waits for them, and re-layouts  66.3 us (20%)
  blocking collectives  49.2 us (15%)
  matrix products  25.5 us (8%)
  between operations  14.3 us (4%)
  other arithmetic  6.4 us (2%)
    reduce_scatter x1, waiting for transfers between devices, shards(): lax.psum_scatter(whole_term, 'feeder', scatter_dimension=0, tiled=True)  91.1 us
    psum x1, waiting for transfers between devices, shards(): variance = lax.psum(variance, 'factor')  71 us
    gather x8, local copies, waits for them, and re-layouts, shards(): sens_rows = jnp.take(sensitivity[member], ev_node[member, interval], axis=0)  61 us
    all_gather x1, blocking collectives, shards(): shard_rows = lax.all_gather(packed, 'feeder', axis=0, tiled=True)  49.2 us
    dot_general x8, matrix products, shards(): jnp.dot(weighted.T, sens_rows, preferred_element_type=jnp.float32)  13.7 us
    dot_general x8, matrix products, shards(): jnp.dot(rows_list[position], volt_grad.T, preferred_element_type=jnp.floa...  11.4 us
  transfers between devices with their start and end apart: 2, of which 2 were waited for; matrix products, arithmetic and copies ran while one was open for 0% of the time, Pallas kernels for 0%

commit v1 on v0

--- a/solution.py
+++ b/solution.py
@@ -9,6 +9,10 @@
 
 
 def shards(sensitivity, headroom, ev_power, ev_node, region_map, loadings):
+
+    def numbers_search(local_array):
+        return lax.all_gather(local_array, axis_name="factor").sum(axis=0)
+
     members = sensitivity.shape[0]
     ev_count = ev_power.shape[2]
     reg_local, hours, columns = loadings.shape
@@ -36,7 +40,7 @@
         partial_sum = jnp.sum(factor_volts * factor_volts, axis=0)
         partial_list.append(partial_sum)
     variance = jnp.stack(partial_list, axis=0).reshape(members, hours, -1)
-    variance = lax.psum(variance, "factor")
+    variance = numbers_search(variance)
     deviation = jnp.sqrt(variance + epsilon)
     margin = headroom - quantile * deviation
     violation = jnp.maximum(-margin, 0.0)

time: 325 us -> 272 us (0.84)
  waiting for transfers between devices: 162 us -> 84.2 us
  blocking collectives: 49.2 us -> 77.6 us
    psum x1 -> x0, waiting for transfers between devices: 71 us -> none  [shards(): variance = lax.psum(variance, 'factor')]
    all_gather x0 -> x1, blocking collectives: none -> 28.4 us  [numbers_search(): return lax.all_gather(local_array, axis_name='factor').sum(axis=0)]
    reduce_scatter x1, waiting for transfers between devices: 91.1 us -> 84.1 us  [shards(): lax.psum_scatter(whole_term, 'feeder', scatter_dimension=0, tiled=True)]
  transfers between devices with their start and end apart: 2 -> 1, of which waited for: 2 -> 1; matrix products, arithmetic and copies ran while one was open for 0% -> 0% of each run, Pallas kernels for 0% -> 0%
where the time goes in v1:
time: 272 us; the launch traced here: 271 us
  waiting for transfers between devices  84.2 us (31%)
  blocking collectives  77.6 us (29%)
  local copies, waits for them, and re-layouts  65.7 us (24%)
  matrix products  24.1 us (9%)
  between operations  14.4 us (5%)
  other arithmetic  5.47 us (2%)
    reduce_scatter x1, waiting for transfers between devices, shards(): lax.psum_scatter(whole_term, 'feeder', scatter_dimension=0, tiled=True)  84.1 us
    gather x8, local copies, waits for them, and re-layouts, shards(): sens_rows = jnp.take(sensitivity[member], ev_node[member, interval], axis=0)  61 us
    all_gather x1, blocking collectives, shards(): shard_rows = lax.all_gather(packed, 'feeder', axis=0, tiled=True)  49.2 us
    all_gather x1, blocking collectives, numbers_search(): return lax.all_gather(local_array, axis_name='factor').sum(axis=0)  28.4 us
    dot_general x8, matrix products, shards(): jnp.dot(weighted.T, sens_rows, preferred_element_type=jnp.float32)  13.7 us
    dot_general x8, matrix products, shards(): jnp.dot(rows_list[position], volt_grad.T, preferred_element_type=jnp.floa...  10 us
  transfers between devices with their start and end apart: 1, of which 1 were waited for; matrix products, arithmetic and copies ran while one was open for 0% of the time, Pallas kernels for 0%

profile of v1, /device:TPU:2, one launch (start us, length us, event | category | flops | bytes accessed | tf_op | source)
XLA Modules:
  0.0 271.4 jit_solution(8871865781920652759)
XLA Ops:
  7.2 1.0 fusion.61
  8.4 1.0 fusion.60
  9.4 0.8 convert_element_type.52
  10.4 49.2 %all_gather.6 = bf16[512,512]{1,0:T(8,128)(2,1)S(1)} all-gather(bf16[16,512]{1,0:T(8,128)(2,1)S(1)} %reshape.159), channel_id=1, replica_groups=mesh['feeder'=32,'factor'=8] {'feeder'}, dimensions={0}, use_global_device_ids=true | all-gather | bytes 540672 | tf_op jit(solution)/shard_map/all_gather | solution.py:22
  59.6 6.8 %gather_fusion.2 = bf16[256,2048]{1,0:T(8,128)(2,1)S(1)} fusion(bf16[2048,2048]{1,0:T(8,128)(2,1)} %bitcast.45, s32[1024]{0:T(1024)S(1)} %pad_clamp_fusion.5), kind=kCustom, calls=%fused_computation.2.clone | custom fusion | bytes 2098176 | tf_op jit(solution)/shard_map/jit(_take)/gather | solution.py:36
  66.4 6.8 %gather_fusion.3 = bf16[256,2048]{1,0:T(8,128)(2,1)S(1)} fusion(bf16[2048,2048]{1,0:T(8,128)(2,1)} %bitcast.46, s32[1024]{0:T(1024)S(1)} %pad_clamp_fusion.4), kind=kCustom, calls=%fused_computation.3.clone | custom fusion | bytes 2098176 | tf_op jit(solution)/shard_map/jit(_take)/gather | solution.py:36
  73.3 7.8 %gather_fusion.4 = bf16[256,2048]{1,0:T(8,128)(2,1)} fusion(bf16[2048,2048]{1,0:T(8,128)(2,1)} %bitcast.47, s32[1024]{0:T(1024)S(1)} %pad_clamp_fusion.3), kind=kCustom, calls=%fused_computation.4.clone | custom fusion | bytes 2098176 | tf_op jit(solution)/shard_map/jit(_take)/gather | solution.py:36
  81.1 8.0 %gather_fusion.5 = bf16[256,2048]{1,0:T(8,128)(2,1)} fusion(bf16[2048,2048]{1,0:T(8,128)(2,1)} %bitcast.48, s32[1024]{0:T(1024)S(1)} %pad_clamp_fusion.2), kind=kCustom, calls=%fused_computation.5.clone | custom fusion | bytes 2098176 | tf_op jit(solution)/shard_map/jit(_take)/gather | solution.py:36
  89.1 7.8 %gather_fusion.6 = bf16[256,2048]{1,0:T(8,128)(2,1)} fusion(bf16[2048,2048]{1,0:T(8,128)(2,1)} %bitcast.49, s32[1024]{0:T(1024)S(1)} %pad_clamp_fusion.1), kind=kCustom, calls=%fused_computation.6.clone | custom fusion | bytes 2098176 | tf_op jit(solution)/shard_map/jit(_take)/gather | solution.py:36
  96.9 7.8 %gather_fusion.7 = bf16[256,2048]{1,0:T(8,128)(2,1)} fusion(bf16[2048,2048]{1,0:T(8,128)(2,1)} %bitcast.50, s32[1024]{0:T(1024)S(1)} %pad_clamp_fusion), kind=kCustom, calls=%fused_computation.7.clone | custom fusion | bytes 2098176 | tf_op jit(solution)/shard_map/jit(_take)/gather | solution.py:36
  104.7 7.9 %gather_fusion.1 = bf16[256,2048]{1,0:T(8,128)(2,1)} fusion(bf16[2048,2048]{1,0:T(8,128)(2,1)} %bitcast.51, s32[1024]{0:T(1024)S(1)} %pad_clamp_fusion.6), kind=kCustom, calls=%fused_computation.1.clone | custom fusion | bytes 2098176 | tf_op jit(solution)/shard_map/jit(_take)/gather | solution.py:36
  112.6 8.0 %gather_fusion = bf16[256,2048]{1,0:T(8,128)(2,1)} fusion(bf16[2048,2048]{1,0:T(8,128)(2,1)} %bitcast.52, s32[1024]{0:T(1024)S(1)} %pad_clamp_fusion.7), kind=kCustom, calls=%fused_computation.clone | custom fusion | bytes 2098176 | tf_op jit(solution)/shard_map/jit(_take)/gather | solution.py:36
  121.0 1.2 multiply_reduce_fusion.5
  122.3 1.2 multiply_reduce_fusion.4
  123.5 2.5 multiply_reduce_fusion.3
  126.0 2.6 multiply_reduce_fusion.2
  128.6 2.4 multiply_reduce_fusion.1
  131.0 1.3 multiply_reduce_fusion
  132.3 1.3 multiply_reduce_fusion.6
  133.5 1.2 multiply_reduce_fusion.7
  134.9 28.4 %all-gather = f32[64,2048]{1,0:T(8,128)S(1)} all-gather(f32[8,2048]{1,0:T(8,128)S(1)} %stack.35), channel_id=2, replica_groups=mesh['feeder'=32,'factor'=8] {'factor'}, dimensions={0}, use_global_device_ids=true | all-gather | bytes 589824 | tf_op jit(solution)/shard_map/all_gather | solution.py:14
  163.3 0.7 bitcast_multiply_fusion
  164.1 2.0 convolution_multiply_fusion
  166.0 1.8 convolution_multiply_fusion.1
  167.9 2.5 convolution_multiply_fusion.2
  170.4 1.1 convolution_multiply_fusion.3
  171.5 1.1 convolution_multiply_fusion.4
  174.2 1.3 concatenate.3
  175.5 2.3 scatter_custom_fusion
  177.9 1.1 slice.172
  179.0 84.1 %reduce-scatter.2.cloned.1.call-done = f32[16,512]{1,0:T(8,128)} async-done(((f32[512,512]{1,0:T(8,128)}), f32[16,512]{1,0:T(8,128)}) %reduce-scatter.2.cloned.1.call-update) | async-done | bytes 32784 | tf_op jit(solution)/shard_map/reduce_scatter | solution.py:63
  263.1 0.8 broadcast_multiply_fusion
  (65 shorter events, 3.1 us)
Async XLA Ops:
  7.2 255.9 %reduce-scatter.2.cloned.1.call-start = ((), (), s32[]{:S(2)}) async-start(), calls=%async_computation.1 | async-start | bytes 1081344 | tf_op jit(solution)/shard_map/reduce_scatter | solution.py:63
  104.7 15.9 %copy-start.8 = (s32[1,256]{1,0:T(1,128)S(1)}, s32[1,256]{1,0:T(1,128)}, u32[]{:S(2)}) copy-start(s32[1,256]{1,0:T(1,128)} %param.12) | copy-start | bytes 3076
  120.6 10.4 %copy-start.5 = (bf16[256,2048]{1,0:T(8,128)(2,1)S(1)}, bf16[256,2048]{1,0:T(8,128)(2,1)}, u32[]{:S(2)}) copy-start(bf16[256,2048]{1,0:T(8,128)(2,1)} %gather_fusion.7) | copy-start | bytes 3145732
  120.6 11.6 %copy-start.2 = (bf16[256,2048]{1,0:T(8,128)(2,1)S(1)}, bf16[256,2048]{1,0:T(8,128)(2,1)}, u32[]{:S(2)}) copy-start(bf16[256,2048]{1,0:T(8,128)(2,1)} %gather_fusion.1) | copy-start | bytes 3145732
  120.6 12.9 %copy-start = (bf16[256,2048]{1,0:T(8,128)(2,1)S(1)}, bf16[256,2048]{1,0:T(8,128)(2,1)}, u32[]{:S(2)}) copy-start(bf16[256,2048]{1,0:T(8,128)(2,1)} %gather_fusion) | copy-start | bytes 3145732
  120.6 42.7 %copy-start.7 = (f32[1,8,2048]{2,1,0:T(8,128)S(1)}, f32[1,8,2048]{2,1,0:T(8,128)}, u32[]{:S(2)}) copy-start(f32[1,8,2048]{2,1,0:T(8,128)} %param.9) | copy-start | bytes 196612
  134.8 38.4 %copy-start.3 = (bf16[256,2048]{1,0:T(8,128)(2,1)S(1)}, bf16[256,2048]{1,0:T(8,128)(2,1)}, u32[]{:S(2)}) copy-start(bf16[256,2048]{1,0:T(8,128)(2,1)} %gather_fusion.1) | copy-start | bytes 3145732
  134.9 35.5 %copy-start.4 = (bf16[256,2048]{1,0:T(8,128)(2,1)S(1)}, bf16[256,2048]{1,0:T(8,128)(2,1)}, u32[]{:S(2)}) copy-start(bf16[256,2048]{1,0:T(8,128)(2,1)} %gather_fusion.4) | copy-start | bytes 3145732
  134.9 35.5 %copy-start.13 = (f32[64,2048]{1,0:T(8,128)S(1)}, f32[64,2048]{1,0:T(8,128)}, u32[]{:S(2)}) copy-start(f32[64,2048]{1,0:T(8,128)} %get-tuple-element.38) | copy-start | bytes 1572868
  134.9 36.6 %copy-start.11 = (f32[64,2048]{1,0:T(8,128)S(1)}, f32[64,2048]{1,0:T(8,128)}, u32[]{:S(2)}) copy-start(f32[64,2048]{1,0:T(8,128)} %get-tuple-element.36) | copy-start | bytes 1572868
  134.9 37.8 %copy-start.9 = (f32[64,2048]{1,0:T(8,128)S(1)}, f32[64,2048]{1,0:T(8,128)}, u32[]{:S(2)}) copy-start(f32[64,2048]{1,0:T(8,128)} %get-tuple-element.34) | copy-start | bytes 1572868
  134.9 38.3 %copy-start.12 = (f32[64,2048]{1,0:T(8,128)S(1)}, f32[64,2048]{1,0:T(8,128)}, u32[]{:S(2)}) copy-start(f32[64,2048]{1,0:T(8,128)} %get-tuple-element.32) | copy-start | bytes 1572868
  164.1 9.6 %copy-start.1 = (bf16[256,2048]{1,0:T(8,128)(2,1)S(1)}, bf16[256,2048]{1,0:T(8,128)(2,1)}, u32[]{:S(2)}) copy-start(bf16[256,2048]{1,0:T(8,128)(2,1)} %gather_fusion) | copy-start | bytes 3145732
  164.1 9.6 %copy-start.10 = (f32[64,2048]{1,0:T(8,128)S(1)}, f32[64,2048]{1,0:T(8,128)}, u32[]{:S(2)}) copy-start(f32[64,2048]{1,0:T(8,128)} %get-tuple-element.30) | copy-start | bytes 1572868
  170.4 93.6 %copy-start.6 = (f32[16,8,64]{2,1,0:T(8,128)S(1)}, f32[16,8,64]{2,1,0:T(8,128)}, u32[]{:S(2)}) copy-start(f32[16,8,64]{2,1,0:T(8,128)} %param.13) | copy-start | bytes 98308
Sparse Core Ops, SparseCore 0:
  179.1 83.9 reduce-scatter.1
